TPU v7x, 32 devices: a whole 2x2x4 slice. The times are simulated.
32 devices in a mesh: col: 8 (over y, x, core), row: 4 (over z).
Axes of the slice: x: 2, y: 2, z: 4, core: 2. Of those that a mesh axis runs over, the one named last changes fastest.
Arguments:
- p_blocks: bfloat16 [4, 72, 4096], P('row', 'col'), may hold values from -0.5390625 to 0.5390625
- p_slots: int32 [4, 72], P('row', 'col'), may hold values from 0 to 18, as said below
- out_slots: int32 [4, 104], P('row', 'col'), may hold values from 0 to 18, as said below
Outputs:
- purified: float32 [4, 104, 4096], P('row', 'col')
Inputs may be any that keep to these rules, and one draw needn't show every extreme that they name: `p_slots`: on each device the used slots (entries below 18) come first and name distinct positions; the remaining slots hold 18. Each device uses between half of its 9 slots (rounded up) and all of them, and some device uses all. `out_slots`: on each device the used slots (entries below 18) come first and name distinct positions; the remaining slots hold 18. Each device uses between half of its 13 slots (rounded up) and all of them, and some device uses all.
All inputs are finite; a program needn't handle non-finite values.
Results may differ from a plain program's by a relative error of at most 0.0003.
Values may be sent and summed in bfloat16 or wider, within the bound.
No kernel may reach another device: no remote copies, remote signals or barrier semaphores. Data moves between devices by JAX's collectives and lax.ppermute only.
A program may use at most 192 MiB of HBM per device.

v0:
```python
import jax
import jax.numpy as jnp
from jax import lax
from jax.sharding import PartitionSpec as P

BLK = 64
COLS_DEV = 3


def on_device(p_blocks, p_slots, out_slots):
    n_row = lax.axis_size("row")
    n_col = lax.axis_size("col")
    capacity = p_slots.shape[1]
    block_edge = BLK
    area = block_edge * block_edge
    rows_dev = COLS_DEV * n_col // n_row
    cells = rows_dev * COLS_DEV
    blocks_total = rows_dev * n_row
    width = COLS_DEV * block_edge
    height = rows_dev * block_edge
    own_ids = p_slots[0]
    id_row = jnp.zeros((1, area), jnp.bfloat16)
    id_row = id_row.at[0, :capacity].set(own_ids.astype(jnp.bfloat16))
    payload = jnp.concatenate([p_blocks[0], id_row], axis=0)
    down = lax.all_gather(payload, "row", axis=0, tiled=False)
    down_ids = down[:, capacity, :capacity].astype(jnp.int32)
    down_row = jnp.arange(n_row, dtype=jnp.int32)[:, None] * rows_dev + down_ids // COLS_DEV
    down_index = jnp.where(
        down_ids < cells, down_row * COLS_DEV + down_ids % COLS_DEV, blocks_total * COLS_DEV
    )
    column_grid = jnp.zeros((blocks_total * COLS_DEV, area), jnp.bfloat16)
    column_grid = column_grid.at[down_index.reshape(-1)].set(
        down[:, :capacity].reshape(n_row * capacity, area), mode="drop"
    )
    column_panel = (
        column_grid.reshape(blocks_total, COLS_DEV, block_edge, block_edge)
        .transpose(0, 2, 1, 3)
        .reshape(blocks_total * block_edge, width)
    )
    across = lax.all_gather(payload, "col", axis=0, tiled=False)
    across_ids = across[:, capacity, :capacity].astype(jnp.int32)
    across_col = jnp.arange(n_col, dtype=jnp.int32)[:, None] * COLS_DEV + across_ids % COLS_DEV
    across_index = jnp.where(
        across_ids < cells,
        across_ids // COLS_DEV * blocks_total + across_col,
        rows_dev * blocks_total,
    )
    row_grid = jnp.zeros((rows_dev * blocks_total, area), jnp.bfloat16)
    row_grid = row_grid.at[across_index.reshape(-1)].set(
        across[:, :capacity].reshape(n_col * capacity, area), mode="drop"
    )
    row_panel = (
        row_grid.reshape(rows_dev, blocks_total, block_edge, block_edge)
        .transpose(0, 2, 1, 3)
        .reshape(height, blocks_total * block_edge)
    )
    square = jnp.dot(row_panel, column_panel, preferred_element_type=jnp.float32)
    square_panel = lax.all_gather(square, "row", axis=0, tiled=True)
    cube = jnp.dot(
        row_panel.astype(jnp.float32),
        square_panel,
        precision=lax.Precision.HIGHEST,
        preferred_element_type=jnp.float32,
    )
    combined = 3.0 * square - 2.0 * cube
    new_grid = combined.reshape(rows_dev, block_edge, COLS_DEV, block_edge).transpose(0, 2, 1, 3)
    new_grid = new_grid.reshape(cells, area)
    out_ids = out_slots[0]
    picked = new_grid[jnp.minimum(out_ids, cells - 1)]
    picked = jnp.where((out_ids < cells)[:, None], picked, jnp.zeros_like(picked))
    return picked[None]


def solution(mesh):
    in_specs = (P("row", "col", None), P("row", "col"), P("row", "col"))
    out_specs = P("row", "col", None)
    return jax.shard_map(
        on_device, mesh=mesh, in_specs=in_specs, out_specs=out_specs, check_vma=False
    )
```

profile of v0, /device:TPU:0, one launch (start us, length us, event | category | flops | bytes accessed | tf_op | source)
XLA Modules:
  0.0 100.4 jit_solution(6214441134641464494)
XLA Ops:
  6.5 0.6 compare_reduce_fusion.4
  7.2 1.3 %broadcast_select_fusion = bf16[1,9]{1,0:T(2,128)(2,1)S(1)} fusion(pred[]{:T(512)} %compare_reduce_fusion.4, s32[1,9]{1,0:T(1,128)} %param.6), kind=kLoop, calls=%fused_computation.34 | loop fusion | flops 18 | bytes 55 | tf_op jit(solution)/shard_map/select.3
  8.5 0.9 fusion.7
  9.4 12.4 %all-gather.2 = bf16[8,10,4096]{2,1,0:T(8,128)(2,1)S(1)} all-gather(bf16[1,10,4096]{2,1,0:T(8,128)(2,1)S(1)} %fusion.7), channel_id=2, replica_groups=mesh['col'=8,'row'=4] {'col'}, dimensions={0}, use_global_device_ids=true | all-gather | bytes 737280 | tf_op jit(solution)/shard_map/all_gather | solution.py:40
  21.9 16.3 %all-gather.3 = bf16[4,10,4096]{2,1,0:T(8,128)(2,1)S(1)} all-gather(bf16[1,10,4096]{2,1,0:T(8,128)(2,1)S(1)} %fusion.7), channel_id=3, replica_groups=mesh['col'=8,'row'=4] {'row'}, dimensions={0}, use_global_device_ids=true | all-gather | bytes 409600 | tf_op jit(solution)/shard_map/all_gather | solution.py:25
  38.3 0.8 copy-done
  39.1 0.5 compare_reduce_fusion.2
  39.8 0.1 lt.92
  39.9 0.1 ne.104
  40.1 0.3 reshape.316
  40.4 1.8 %scatter_custom_fusion = bf16[144,4096]{1,0:T(8,128)(2,1)S(1)} fusion(s32[72]{0:T(128)S(1)} %fusion.12, bf16[72,4096]{1,0:T(8,128)(2,1)S(1)} %reshape.316, bf16[]{:T(256)} %constant.75.clone.1), kind=kCustom, calls=%fused_computation.5 | custom fusion | bytes 1179650 | tf_op jit(solution)/shard_map/scatter | solution.py:49
  42.2 2.6 %reshape.297 = bf16[6,24,64,64]{3,2,1,0:T(8,128)(2,1)S(1)} reshape(bf16[144,4096]{1,0:T(8,128)(2,1)S(1)} %scatter_custom_fusion) | data formatting | bytes 2359296 | tf_op jit(solution)/shard_map/reshape | solution.py:53
  44.8 2.9 %copy.12 = bf16[6,64,24,64]{3,2,1,0:T(8,128)(2,1)} copy(bf16[6,64,24,64]{3,1,2,0:T(8,128)(2,1)S(1)} %bitcast.34) | data formatting | bytes 2359296 | tf_op jit(solution)/shard_map/transpose | solution.py:54
  47.7 3.5 %reshape.298 = bf16[384,1536]{1,0:T(8,128)(2,1)S(1)} reshape(bf16[6,64,24,64]{3,2,1,0:T(8,128)(2,1)} %copy.12) | data formatting | bytes 2359296 | tf_op jit(solution)/shard_map/reshape | solution.py:55
  51.3 0.1 div.37
  51.4 0.1 lt.97
  51.5 0.1 ne.109
  51.7 0.1 add.147
  51.8 0.1 reshape.324
  51.9 1.2 %scatter_custom_fusion.1 = bf16[72,4096]{1,0:T(8,128)(2,1)S(1)} fusion(s32[36]{0:T(128)S(1)} %fusion.13, bf16[36,4096]{1,0:T(8,128)(2,1)S(1)} %reshape.324, bf16[]{:T(256)} %constant.75.clone.1), kind=kCustom, calls=%fused_computation.7 | custom fusion | bytes 589826 | tf_op jit(solution)/shard_map/scatter | solution.py:32
  53.1 1.3 %reshape.300 = bf16[24,3,64,64]{3,2,1,0:T(8,128)(2,1)S(1)} reshape(bf16[72,4096]{1,0:T(8,128)(2,1)S(1)} %scatter_custom_fusion.1) | data formatting | bytes 1179648 | tf_op jit(solution)/shard_map/reshape | solution.py:36
  54.4 1.3 %copy.13 = bf16[24,64,3,64]{1,0,3,2:T(8,128)(2,1)S(1)} copy(bf16[24,64,3,64]{3,1,2,0:T(8,128)(2,1)S(1)} %bitcast.35) | data formatting | bytes 1179648 | tf_op jit(solution)/shard_map/transpose | solution.py:37
  55.7 0.7 reshape.301
  56.4 1.3 %fusion.15 = f32[384,192]{0,1:T(8,128)} fusion(bf16[384,1536]{1,0:T(8,128)(2,1)S(1)} %reshape.298, bf16[1536,192]{0,1:T(8,128)(2,1)S(1)} %reshape.301), kind=kOutput, calls=%fused_computation.44 | convolution fusion | flops 226492416 | bytes 2064384 | tf_op jit(solution)/shard_map/dot_general | solution.py:57
  57.8 30.9 %all-gather.6.cloned.1.call-done = f32[1536,192]{0,1:T(8,128)} async-done(((f32[384,192]{0,1:T(8,128)}), f32[1536,192]{0,1:T(8,128)}) %all-gather.6.cloned.1.call-update) | async-done | bytes 1179664 | tf_op jit(solution)/shard_map/all_gather | solution.py:58
  88.7 2.6 %fusion = f32[384,192]{0,1:T(8,128)S(1)} fusion(bf16[384,1536]{1,0:T(8,128)(2,1)S(1)} %reshape.298, f32[1536,192]{0,1:T(8,128)} %all-gather.6.cloned.1.call-done, f32[384,192]{0,1:T(8,128)} %fusion.15), kind=kOutput, calls=%fused_computation.4 | convolution fusion | flops 1359175680 | bytes 2949120 | tf_op jit(solution)/shard_map/dot_general | solution.py:59
  91.3 0.2 reshape.302
  91.4 0.3 copy.14
  91.7 0.2 reshape.303
  91.9 0.6 gather_fusion
  92.5 0.1 bitcast_select_fusion
  92.6 0.9 copy.15
  (25 shorter events, 0.7 us)
Async XLA Ops:
  6.5 82.2 %all-gather.6.cloned.1.call-start = ((), (), s32[]{:S(2)}) async-start(), calls=%async_computation | async-start | bytes 1474560 | tf_op jit(solution)/shard_map/all_gather | solution.py:58
  38.3 0.8 copy-start
  47.7 3.7 %copy-start.2 = (pred[4,9]{1,0:T(4,128)(4,1)S(1)}, pred[4,9]{1,0:T(4,128)(4,1)}, u32[]{:S(2)}) copy-start(pred[4,9]{1,0:T(4,128)(4,1)} %get-tuple-element.22) | copy-start | bytes 112
  47.7 4.0 %copy-start.1 = (bf16[4,10,4096]{2,1,0:T(8,128)(2,1)S(1)}, bf16[4,10,4096]{2,1,0:T(8,128)(2,1)}, u32[]{:S(2)}) copy-start(bf16[4,10,4096]{2,1,0:T(8,128)(2,1)} %copy-done) | copy-start | bytes 983044
  56.4 1.3 %copy-start.3 = (s32[1,13]{1,0:T(1,128)S(1)}, s32[1,13]{1,0:T(1,128)}, u32[]{:S(2)}) copy-start(s32[1,13]{1,0:T(1,128)} %param.7) | copy-start | bytes 160
Sparse Core Ops, SparseCore 0:
  57.9 30.7 all-gather.5
where the time goes:
time: 101 us; the launch traced here: 100 us
  waiting for transfers between devices  30.9 us (31%)
  blocking collectives  28.8 us (29%)
  local copies, waits for them, and re-layouts  19.6 us (19%)
  between operations  13.6 us (13%)
  matrix products  3.83 us (4%)
  other arithmetic  3.67 us (4%)
    all_gather x1, waiting for transfers between devices, on_device(): square_panel = lax.all_gather(square, 'row', axis=0, tiled=True)  30.9 us
    all_gather x1, blocking collectives, on_device(): down = lax.all_gather(payload, 'row', axis=0, tiled=False)  16.3 us
    all_gather x1, blocking collectives, on_device(): across = lax.all_gather(payload, 'col', axis=0, tiled=False)  12.4 us
    reshape x1, local copies, waits for them, and re-layouts, on_device(): row_panel = row_grid.reshape(rows_dev, blocks_total, block_edge, block_ed...  3.5 us
    transpose x1, local copies, waits for them, and re-layouts, on_device(): row_panel = row_grid.reshape(rows_dev, blocks_total, block_edge, block_ed...  2.94 us
    reshape x1, local copies, waits for them, and re-layouts, on_device(): row_grid.reshape(rows_dev, blocks_total, block_edge, block_edge)  2.57 us
    dot_general x1, matrix products, on_device(): jnp.dot(row_panel.astype(jnp.float32), square_panel, precision=lax.Precis...  2.56 us
  transfers between devices with their start and end apart: 1, of which 1 were waited for; matrix products, arithmetic and copies ran while one was open for 0% of the time, Pallas kernels for 0%

commit v1 on v0

--- a/solution.py
+++ b/solution.py
@@ -55,7 +55,21 @@
         .reshape(height, blocks_total * block_edge)
     )
     square = jnp.dot(row_panel, column_panel, preferred_element_type=jnp.float32)
-    square_panel = lax.all_gather(square, "row", axis=0, tiled=True)
+    ways, here, lap = (lax.axis_size("row"), lax.axis_index("row"), square.shape[0])
+    dims = [n * ways if d == 0 else n for d, n in enumerate(square.shape)]
+    full = lax.dynamic_update_slice_in_dim(
+        jnp.zeros(dims, square.dtype), square, here * lap, axis=0
+    )
+    going_up = going_down = square
+    for far in range(1, ways // 2 + 1):
+        going_up = lax.ppermute(going_up, "row", [(d, (d + 1) % ways) for d in range(ways)])
+        full = lax.dynamic_update_slice_in_dim(full, going_up, (here - far) % ways * lap, axis=0)
+        if 2 * far < ways:
+            going_down = lax.ppermute(going_down, "row", [(d, (d - 1) % ways) for d in range(ways)])
+            full = lax.dynamic_update_slice_in_dim(
+                full, going_down, (here + far) % ways * lap, axis=0
+            )
+    square_panel = full
     cube = jnp.dot(
         row_panel.astype(jnp.float32),
         square_panel,

time: 101 us -> 78 us (0.77)
  between operations: 13.6 us -> 0.22 us
  waiting for transfers between devices: 30.9 us -> 18.2 us
  starting transfers between devices: 0.01 us -> 4.01 us
  matrix products: 3.83 us -> 1.79 us
  local copies, waits for them, and re-layouts: 19.6 us -> 21 us
    all_gather x1 -> x0, waiting for transfers between devices: 30.9 us -> none  [on_device(): square_panel = lax.all_gather(square, 'row', axis=0, tiled=True)]
    ppermute x0 -> x3, waiting for transfers between devices: none -> 18.2 us  [the longest x2 14.8 us: on_device(): lax.ppermute(going_up, 'row', [(d, (d + 1) % ways) for d in range(ways)])]
    ppermute x0 -> x3, starting transfers between devices: none -> 4.01 us  [the longest x1 2.04 us: on_device(): lax.ppermute(going_down, 'row', [(d, (d - 1) % ways) for d in range(ways)])]
    dot_general x1, matrix products: 2.56 us -> 1.25 us  [on_device(): jnp.dot(row_panel.astype(jnp.float32), square_panel, precision=lax.Precis...]
  transfers between devices with their start and end apart: 1 -> 3, of which waited for: 1 -> 3; matrix products, arithmetic and copies ran while one was open for 0% -> 0% of each run, Pallas kernels for 0% -> 0%
where the time goes in v1:
time: 78 us; the launch traced here: 77.7 us
  blocking collectives  28.8 us (37%)
  local copies, waits for them, and re-layouts  21 us (27%)
  waiting for transfers between devices  18.2 us (23%)
  starting transfers between devices  4.01 us (5%)
  other arithmetic  3.72 us (5%)
  matrix products  1.79 us (2%)
    all_gather x1, blocking collectives, on_device(): down = lax.all_gather(payload, 'row', axis=0, tiled=False)  16.3 us
    ppermute x2, waiting for transfers between devices, on_device(): lax.ppermute(going_up, 'row', [(d, (d + 1) % ways) for d in range(ways)])  14.8 us
    all_gather x1, blocking collectives, on_device(): across = lax.all_gather(payload, 'col', axis=0, tiled=False)  12.4 us
    reshape x1, local copies, waits for them, and re-layouts, on_device(): row_panel = row_grid.reshape(rows_dev, blocks_total, block_edge, block_ed...  3.5 us
    ppermute x1, waiting for transfers between devices, on_device(): lax.ppermute(going_down, 'row', [(d, (d - 1) % ways) for d in range(ways)])  3.33 us
    transpose x1, local copies, waits for them, and re-layouts, on_device(): row_panel = row_grid.reshape(rows_dev, blocks_total, block_edge, block_ed...  2.94 us
    reshape x1, local copies, waits for them, and re-layouts, on_device(): row_grid.reshape(rows_dev, blocks_total, block_edge, block_edge)  2.57 us
    ppermute x1, starting transfers between devices, on_device(): lax.ppermute(going_down, 'row', [(d, (d - 1) % ways) for d in range(ways)])  2.04 us
  transfers between devices with their start and end apart: 3, of which 3 were waited for; matrix products, arithmetic and copies ran while one was open for 0% of the time, Pallas kernels for 0%

profile of v1, /device:TPU:0, one launch (start us, length us, event | category | flops | bytes accessed | tf_op | source)
XLA Modules:
  0.0 77.7 jit_solution(1348604308676127025)
XLA Ops:
  0.0 0.6 compare_reduce_fusion.4
  0.6 1.3 %broadcast_select_fusion = bf16[1,9]{1,0:T(2,128)(2,1)S(1)} fusion(pred[]{:T(512)} %compare_reduce_fusion.4, s32[1,9]{1,0:T(1,128)} %param.6), kind=kLoop, calls=%fused_computation.38 | loop fusion | flops 18 | bytes 55 | tf_op jit(solution)/shard_map/select.9
  1.9 0.9 %fusion.7 = bf16[1,10,4096]{2,1,0:T(8,128)(2,1)S(1)} fusion(bf16[1,9]{1,0:T(2,128)(2,1)S(1)} %broadcast_select_fusion, bf16[9,4096]{1,0:T(8,128)(2,1)} %bitcast.39), kind=kLoop, calls=%fused_computation.13 | loop fusion | flops 245760 | bytes 155666
  2.9 12.4 %all-gather.2 = bf16[8,10,4096]{2,1,0:T(8,128)(2,1)S(1)} all-gather(bf16[1,10,4096]{2,1,0:T(8,128)(2,1)S(1)} %fusion.7), channel_id=2, replica_groups=mesh['col'=8,'row'=4] {'col'}, dimensions={0}, use_global_device_ids=true | all-gather | bytes 737280 | tf_op jit(solution)/shard_map/all_gather | solution.py:40
  15.4 16.3 %all-gather.3 = bf16[4,10,4096]{2,1,0:T(8,128)(2,1)S(1)} all-gather(bf16[1,10,4096]{2,1,0:T(8,128)(2,1)S(1)} %fusion.7), channel_id=3, replica_groups=mesh['col'=8,'row'=4] {'row'}, dimensions={0}, use_global_device_ids=true | all-gather | bytes 409600 | tf_op jit(solution)/shard_map/all_gather | solution.py:25
  31.7 0.6 compare_reduce_fusion.2
  32.3 0.2 copy-done.1
  33.1 0.3 reshape.316
  33.4 1.8 %scatter_custom_fusion = bf16[144,4096]{1,0:T(8,128)(2,1)S(1)} fusion(s32[72]{0:T(128)S(1)} %fusion.12, bf16[72,4096]{1,0:T(8,128)(2,1)S(1)} %reshape.316, bf16[]{:T(256)} %constant.104.clone.1), kind=kCustom, calls=%fused_computation.5 | custom fusion | bytes 1179650 | tf_op jit(solution)/shard_map/scatter | solution.py:49
  35.2 2.6 %reshape.297 = bf16[6,24,64,64]{3,2,1,0:T(8,128)(2,1)S(1)} reshape(bf16[144,4096]{1,0:T(8,128)(2,1)S(1)} %scatter_custom_fusion) | data formatting | bytes 2359296 | tf_op jit(solution)/shard_map/reshape | solution.py:53
  37.8 2.9 %copy.12 = bf16[6,64,24,64]{3,2,1,0:T(8,128)(2,1)} copy(bf16[6,64,24,64]{3,1,2,0:T(8,128)(2,1)S(1)} %bitcast.34) | data formatting | bytes 2359296 | tf_op jit(solution)/shard_map/transpose | solution.py:54
  40.7 3.5 %reshape.298 = bf16[384,1536]{1,0:T(8,128)(2,1)S(1)} reshape(bf16[6,64,24,64]{3,2,1,0:T(8,128)(2,1)} %copy.12) | data formatting | bytes 2359296 | tf_op jit(solution)/shard_map/reshape | solution.py:55
  44.7 0.1 reshape.324
  44.9 1.2 %scatter_custom_fusion.1 = bf16[72,4096]{1,0:T(8,128)(2,1)S(1)} fusion(s32[36]{0:T(128)S(1)} %fusion.13, bf16[36,4096]{1,0:T(8,128)(2,1)S(1)} %reshape.324, bf16[]{:T(256)} %constant.104.clone.1), kind=kCustom, calls=%fused_computation.7 | custom fusion | bytes 589826 | tf_op jit(solution)/shard_map/scatter | solution.py:32
  46.1 1.3 %reshape.300 = bf16[24,3,64,64]{3,2,1,0:T(8,128)(2,1)S(1)} reshape(bf16[72,4096]{1,0:T(8,128)(2,1)S(1)} %scatter_custom_fusion.1) | data formatting | bytes 1179648 | tf_op jit(solution)/shard_map/reshape | solution.py:36
  47.4 1.3 %copy.13 = bf16[24,64,3,64]{1,0,3,2:T(8,128)(2,1)S(1)} copy(bf16[24,64,3,64]{3,1,2,0:T(8,128)(2,1)S(1)} %bitcast.35) | data formatting | bytes 1179648 | tf_op jit(solution)/shard_map/transpose | solution.py:37
  48.7 1.5 %reshape.301 = bf16[1536,192]{0,1:T(8,128)(2,1)} reshape(bf16[24,64,3,64]{1,0,3,2:T(8,128)(2,1)S(1)} %copy.13) | data formatting | bytes 1179648 | tf_op jit(solution)/shard_map/reshape | solution.py:38
  50.2 0.1 broadcast_in_dim.41
  50.3 0.9 %copy-done = bf16[1536,192]{0,1:T(8,128)(2,1)S(1)} copy-done((bf16[1536,192]{0,1:T(8,128)(2,1)S(1)}, bf16[1536,192]{0,1:T(8,128)(2,1)}, u32[]{:S(2)}) %copy-start) | copy-done | bytes 589848
  51.3 0.5 constant_dynamic-update-slice_fusion.3
  51.8 1.9 %collective-permute-start = (f32[384,192]{0,1:T(8,128)S(1)}, f32[384,192]{0,1:T(8,128)S(1)}, u32[]{:S(2)}, u32[]{:S(2)}) collective-permute-start(f32[384,192]{0,1:T(8,128)S(1)} %get-tuple-element.26), channel_id=1, source_target_pairs={{0,1},{1,2},{2,3},{3,0},{4,5},{5,6},{6,7},{7,4},{8,9},{9,10},{10,1... | collective-permute-start | bytes 884744 | tf_op jit(solution)/shard_map/ppermute | solution.py:65
  53.8 2.0 %collective-permute-start.1 = (f32[384,192]{0,1:T(8,128)S(1)}, f32[384,192]{0,1:T(8,128)S(1)}, u32[]{:S(2)}, u32[]{:S(2)}) collective-permute-start(f32[384,192]{0,1:T(8,128)S(1)} %get-tuple-element.26), channel_id=1, source_target_pairs={{0,3},{1,0},{2,1},{3,2},{4,7},{5,4},{6,5},{7,6},{8,11},{9,8},{10,9... | collective-permute-start | bytes 884744 | tf_op jit(solution)/shard_map/ppermute | solution.py:68
  55.8 7.8 %collective-permute-done = f32[384,192]{0,1:T(8,128)S(1)} collective-permute-done((f32[384,192]{0,1:T(8,128)S(1)}, f32[384,192]{0,1:T(8,128)S(1)}, u32[]{:S(2)}, u32[]{:S(2)}) %collective-permute-start) | collective-permute-done | bytes 294944 | tf_op jit(solution)/shard_map/ppermute | solution.py:65
  63.7 3.3 %collective-permute-done.1 = f32[384,192]{0,1:T(8,128)S(1)} collective-permute-done((f32[384,192]{0,1:T(8,128)S(1)}, f32[384,192]{0,1:T(8,128)S(1)}, u32[]{:S(2)}, u32[]{:S(2)}) %collective-permute-start.1) | collective-permute-done | bytes 294944 | tf_op jit(solution)/shard_map/ppermute | solution.py:68
  67.1 7.1 %collective-permute-done.2 = f32[384,192]{0,1:T(8,128)S(1)} collective-permute-done((f32[384,192]{0,1:T(8,128)S(1)}, f32[384,192]{0,1:T(8,128)S(1)}, u32[]{:S(2)}, u32[]{:S(2)}) %collective-permute-start.2) | collective-permute-done | bytes 294944 | tf_op jit(solution)/shard_map/ppermute | solution.py:65
  74.2 1.2 %fusion = f32[384,192]{0,1:T(8,128)S(1)} fusion(bf16[384,1536]{1,0:T(8,128)(2,1)S(1)} %reshape.298, f32[1536,192]{0,1:T(8,128)S(1)} %constant_dynamic-update-slice_fusion, f32[384,192]{0,1:T(8,128)S(1)} %get-tuple-element.26), kind=kOutput, calls=%fused_computation.4 | convolution fusion | flops 1359175680 | bytes 2949120 | tf_op jit(solution)/shard_map/dot_general | solution.py:73
  75.4 0.2 reshape.302
  75.6 0.3 copy.14
  75.9 0.2 reshape.303
  76.1 0.6 gather_fusion
  76.7 0.1 bitcast_select_fusion
  76.8 0.9 %copy.15 = f32[1,13,4096]{2,0,1:T(1,128)} copy(f32[1,13,4096]{2,1,0:T(8,128)S(1)} %bitcast_select_fusion) | data formatting | bytes 425984 | tf_op jit(solution)/shard_map/jit(_where)/select_n | solution.py:84
  (34 shorter events, 1.3 us)
Async XLA Ops:
  31.7 0.8 %copy-start.1 = (bf16[4,10,4096]{2,1,0:T(8,128)(2,1)}, bf16[4,10,4096]{2,1,0:T(8,128)(2,1)S(1)}, u32[]{:S(2)}) copy-start(bf16[4,10,4096]{2,1,0:T(8,128)(2,1)S(1)} %all-gather.3) | copy-start | bytes 983044
  40.7 3.5 %copy-start.3 = (pred[4,9]{1,0:T(4,128)(4,1)S(1)}, pred[4,9]{1,0:T(4,128)(4,1)}, u32[]{:S(2)}) copy-start(pred[4,9]{1,0:T(4,128)(4,1)} %get-tuple-element.22) | copy-start | bytes 112
  40.7 4.0 %copy-start.2 = (bf16[4,10,4096]{2,1,0:T(8,128)(2,1)S(1)}, bf16[4,10,4096]{2,1,0:T(8,128)(2,1)}, u32[]{:S(2)}) copy-start(bf16[4,10,4096]{2,1,0:T(8,128)(2,1)} %copy-done.1) | copy-start | bytes 983044
  50.2 1.1 %copy-start = (bf16[1536,192]{0,1:T(8,128)(2,1)S(1)}, bf16[1536,192]{0,1:T(8,128)(2,1)}, u32[]{:S(2)}) copy-start(bf16[1536,192]{0,1:T(8,128)(2,1)} %reshape.301) | copy-start | bytes 1769476
  51.3 4.5 %copy-start.4 = (s32[1,13]{1,0:T(1,128)S(1)}, s32[1,13]{1,0:T(1,128)}, u32[]{:S(2)}) copy-start(s32[1,13]{1,0:T(1,128)} %param.7) | copy-start | bytes 160
  51.8 11.8 %collective-permute-start = (f32[384,192]{0,1:T(8,128)S(1)}, f32[384,192]{0,1:T(8,128)S(1)}, u32[]{:S(2)}, u32[]{:S(2)}) collective-permute-start(f32[384,192]{0,1:T(8,128)S(1)} %get-tuple-element.26), channel_id=1, source_target_pairs={{0,1},{1,2},{2,3},{3,0},{4,5},{5,6},{6,7},{7,4},{8,9},{9,10},{10,1... | collective-permute-start | bytes 884744 | tf_op jit(solution)/shard_map/ppermute | solution.py:65
  53.8 13.3 %collective-permute-start.1 = (f32[384,192]{0,1:T(8,128)S(1)}, f32[384,192]{0,1:T(8,128)S(1)}, u32[]{:S(2)}, u32[]{:S(2)}) collective-permute-start(f32[384,192]{0,1:T(8,128)S(1)} %get-tuple-element.26), channel_id=1, source_target_pairs={{0,3},{1,0},{2,1},{3,2},{4,7},{5,4},{6,5},{7,6},{8,11},{9,8},{10,9... | collective-permute-start | bytes 884744 | tf_op jit(solution)/shard_map/ppermute | solution.py:68
  63.6 10.5 %collective-permute-start.2 = (f32[384,192]{0,1:T(8,128)S(1)}, f32[384,192]{0,1:T(8,128)S(1)}, u32[]{:S(2)}, u32[]{:S(2)}) collective-permute-start(f32[384,192]{0,1:T(8,128)S(1)} %collective-permute-done), channel_id=1, source_target_pairs={{0,1},{1,2},{2,3},{3,0},{4,5},{5,6},{6,7},{7,4},{8,9},{9,10},{10,1... | collective-permute-start | bytes 884744 | tf_op jit(solution)/shard_map/ppermute | solution.py:65
